TPU v7x, 256 devices: a whole 4x4x8 slice. The times are simulated.
256 devices in a mesh: rep: 16 (over z_lo, x), shard: 16 (over z_hi, y, core).
Axes of the slice: x: 4, y: 4, z: 8 (z_hi: 2, z_lo: 4; z = z_hi * 4 + z_lo), core: 2. Of those that a mesh axis runs over, the one named last changes fastest.
Arguments:
- attn: bfloat16 [16, 6144, 2560], P('rep', 'shard'), may hold values from -6 to 6
- resid: bfloat16 [16, 6144, 2560], P('rep', 'shard'), may hold values from -200 to 200
- cotangent: bfloat16 [16, 6144, 2560], P('rep', 'shard'), may hold values from -6 to 6
- gain: float32 [2560], replicated, may hold values from 0.1 to 1.9
- numer: float32 [16, 2560, 2560], P('rep', 'shard'), may hold values from -6 to 6
- pweight: float32 [16], P('rep'), may hold values from 0.5 to 2
- round_bit: int32 [1], replicated, may hold values from 0 to 3
Outputs:
- new_numer: float32 [16, 2560, 2560], P('rep', 'shard')
- new_pweight: float32 [16], P('rep')
All inputs are finite; a program needn't handle non-finite values.
Results may differ from a plain program's by a relative error of at most 0.008.
Values may be sent and summed in bfloat16 or wider, within the bound.
No kernel may reach another device: no remote copies, remote signals or barrier semaphores. Data moves between devices by JAX's collectives and lax.ppermute only.
A program may use at most 192 MiB of HBM per device.

v0:
```python
import jax
import jax.numpy as jnp
from jax import lax
from jax.sharding import PartitionSpec as P

EPS = 1e-05
learning_rate = 0.5


def shortened(shard):

    def short(part):
        return part.astype(jnp.bfloat16) if part.dtype == jnp.float32 else part

    return jax.tree.map(short, shard)


def from_partner(shard, axis, apart):
    return lax.ppermute(shard, axis, [(i, i ^ 1 << apart) for i in range(lax.axis_size(axis))])


def on_device(attn, resid, cotangent, gain, numer, pweight, round_bit):
    acts = attn[0]
    weight_rows = (numer[0] / pweight[0]).astype(jnp.bfloat16)
    columns = acts
    pre = resid[0].astype(jnp.float32) + jnp.dot(
        columns,
        lax.all_gather(weight_rows, "shard", axis=0, tiled=True),
        preferred_element_type=jnp.float32,
    )
    inv = lax.rsqrt(jnp.mean(pre * pre, axis=1, keepdims=True) + EPS)
    normed = pre * inv
    dnorm = cotangent[0].astype(jnp.float32) * gain
    dpre = (inv * (dnorm - normed * jnp.mean(dnorm * normed, axis=1, keepdims=True))).astype(
        jnp.bfloat16
    )
    columns = acts
    grad = lax.psum_scatter(
        lax.dot_general(
            columns, dpre, (((0,), (0,)), ((), ())), preferred_element_type=jnp.float32
        ).astype(jnp.bfloat16),
        "shard",
        scatter_dimension=0,
        tiled=True,
    ).astype(jnp.float32)
    stepped = numer[0] - learning_rate * grad
    levels = lax.axis_size("rep").bit_length() - 1

    def pushed(bit):

        def send_pair(pair):
            return jax.tree.map(
                lambda part, own: part.astype(own.dtype),
                from_partner(shortened(pair), "rep", bit),
                pair,
            )

        return send_pair

    other_numer, other_weight = lax.switch(
        round_bit[0], [pushed(level) for level in range(levels)], (stepped, pweight)
    )
    new_numer = (0.5 * (stepped + other_numer))[None]
    new_pweight = 0.5 * (pweight + other_weight)
    return (new_numer, new_pweight)


def solution(mesh):
    in_specs = (
        P("rep", "shard", None),
        P("rep", "shard", None),
        P("rep", "shard", None),
        P(),
        P("rep", "shard", None),
        P("rep"),
        P(),
    )
    out_specs = (P("rep", "shard", None), P("rep"))
    return jax.shard_map(
        on_device, mesh=mesh, in_specs=in_specs, out_specs=out_specs, check_vma=False
    )
```

profile of v0, /device:TPU:32, one launch (start us, length us, event | category | flops | bytes accessed | tf_op | source)
XLA Modules:
  0.0 410.0 jit_solution(1422949947530526747)
XLA Ops:
  7.2 0.0 copy-start
  7.2 0.0 all-gather.2.cloned.1.call-start
  8.0 2.4 fusion.14
  10.4 0.0 all-gather.2.cloned.1.call-update
  10.5 0.0 reduce-scatter.4.cloned.1.call-start
  10.5 4.0 copy.18
  14.5 4.0 copy.19
  18.5 139.0 %all-gather.2.cloned.1.call-done = bf16[2560,2560]{1,0:T(8,128)(2,1)} async-done(((bf16[160,2560]{1,0:T(8,128)(2,1)}), bf16[2560,2560]{1,0:T(8,128)(2,1)}) %all-gather.2.cloned.1.call-update) | async-done | bytes 13107216 | tf_op jit(solution)/shard_map/all_gather | solution.py:28
  157.5 10.8 %multiply_reduce_fusion = (f32[384]{0:T(512)S(1)}, f32[384,2560]{0,1:T(8,128)S(1)}) fusion(bf16[2560,2560]{1,0:T(8,128)(2,1)} %all-gather.2.cloned.1.call-done, bf16[1,384,2560]{2,1,0:T(8,128)(2,1)S(1)} %copy-done, bf16[1,384,2560]{1,2,0:T(8,128)(2,1)} %copy.18), kind=kOutput, calls=%fused_computation.10 | convolution fusion | flops 5037096448 | bytes 20973056 | tf_op jit(solution)/shard_map/dot_general | solution.py:26
  168.3 0.7 fusion.4
  169.0 10.4 %fusion = bf16[2560,2560]{0,1:T(8,128)(2,1)} fusion(f32[384,2560]{0,1:T(8,128)S(1)} %get-tuple-element.59, bf16[1,384,2560]{1,2,0:T(8,128)(2,1)S(1)} %copy-done.2, bf16[1,384,2560]{2,1,0:T(8,128)(2,1)S(1)} %copy-done, f32[384]{0:T(512)S(1)} %broadcast_multiply_fusion, f32[2560]{0:T(1024)S(1)} %copy-done.4, f32[384]{0:T(512)S(1)} %add_rsqrt_fusion), kind=kOutput, calls=%fused_computation.1 | convolution fusion | flops 5046599680 | bytes 20984832 | tf_op jit(solution)/shard_map/dot_general | solution.py:39
  179.5 17.6 %copy.21 = bf16[2560,2560]{1,0:T(8,128)(2,1)} copy(bf16[2560,2560]{0,1:T(8,128)(2,1)} %fusion) | data formatting | bytes 26214400
  197.1 0.0 reduce-scatter.4.cloned.1.call-update
  197.9 175.3 %reduce-scatter.4.cloned.1.call-done = bf16[160,2560]{1,0:T(8,128)(2,1)} async-done(((bf16[2560,2560]{1,0:T(8,128)(2,1)}), bf16[160,2560]{1,0:T(8,128)(2,1)}) %reduce-scatter.4.cloned.1.call-update) | async-done | bytes 819216 | tf_op jit(solution)/shard_map/reduce_scatter | solution.py:38
  373.2 2.5 bitcast_subtract_fusion
  375.7 23.0 %conditional.4 = (f32[160,2560]{1,0:T(8,128)}, f32[1]{0:T(128)}) conditional(s32[]{:T(128)} %bitcast.7, (f32[160,2560]{1,0:T(8,128)}, f32[1]{0:T(128)}) %tuple.50, (f32[160,2560]{1,0:T(8,128)}, f32[1]{0:T(128)}) %tuple.50, (f32[160,2560]{1,0:T(8,128)}, f32[1]{0:T(128)}) %tuple.50, (f32[160,2560]{1,0:T(8,128)}, ...), branch_computations={%region_3.0_spmd, %region_4.0_spmd, %region_5.0_spmd, %region_6.0_... | conditional | flops 819202 | bytes 8192116
  375.7 1.5 convert_element_type.70
  377.2 1.6 collective-permute-start
  379.4 16.2 %collective-permute-start.1 = (bf16[1]{0:T(256)(128)(2,1)}, bf16[1]{0:T(256)(128)(2,1)}, u32[]{:S(2)}, u32[]{:S(2)}) collective-permute-start(bf16[1]{0:T(256)(128)(2,1)} %convert_element_type.72), channel_id=1, source_target_pairs={{0,16},{16,0},{32,48},{48,32},{64,80},{80,64},{96,112},{112,96},{1... | collective-permute-start | bytes 14 | tf_op jit(solution)/shard_map/cond/branch_0_fun/ppermute | solution.py:19
  395.6 1.1 collective-permute-done.1
  397.3 0.0 collective-permute-done
  397.3 1.4 convert_element_type.108
  398.7 3.4 multiply_bitcast_fusion
  402.1 0.0 copy-done.1
  (10 shorter events, 0.0 us)
Async XLA Ops:
  7.2 150.3 %copy-start = (bf16[1,384,2560]{2,1,0:T(8,128)(2,1)S(1)}, bf16[1,384,2560]{2,1,0:T(8,128)(2,1)}, u32[]{:S(2)}) copy-start(bf16[1,384,2560]{2,1,0:T(8,128)(2,1)} %param.11) | copy-start | bytes 5898244
  7.2 150.3 %all-gather.2.cloned.1.call-start = ((), (), s32[]{:S(2)}) async-start(), calls=%async_computation.1 | async-start | bytes 13926400 | tf_op jit(solution)/shard_map/all_gather | solution.py:28
  10.5 362.7 %reduce-scatter.4.cloned.1.call-start = ((), (), s32[]{:S(2)}) async-start(), calls=%async_computation.2 | async-start | bytes 13926400 | tf_op jit(solution)/shard_map/reduce_scatter | solution.py:38
  18.5 149.8 %copy-start.4 = (f32[2560]{0:T(1024)S(1)}, f32[2560]{0:T(1024)}, u32[]{:S(2)}) copy-start(f32[2560]{0:T(1024)} %param.14) | copy-start | bytes 30724
  157.5 10.8 %copy-start.2 = (bf16[1,384,2560]{1,2,0:T(8,128)(2,1)S(1)}, bf16[1,384,2560]{1,2,0:T(8,128)(2,1)}, u32[]{:S(2)}) copy-start(bf16[1,384,2560]{1,2,0:T(8,128)(2,1)} %copy.19) | copy-start | bytes 5898244
  197.1 176.1 %copy-start.3 = (f32[1,160,2560]{2,1,0:T(8,128)S(1)}, f32[1,160,2560]{2,1,0:T(8,128)}, u32[]{:S(2)}) copy-start(f32[1,160,2560]{2,1,0:T(8,128)} %param.15) | copy-start | bytes 4915204
  377.2 20.1 %collective-permute-start = (bf16[160,2560]{1,0:T(8,128)(2,1)S(1)}, bf16[160,2560]{1,0:T(8,128)(2,1)S(1)}, u32[]{:S(2)}, u32[]{:S(2)}) collective-permute-start(bf16[160,2560]{1,0:T(8,128)(2,1)S(1)} %convert_element_type.70), channel_id=1, source_target_pairs={{0,16},{16,0},{32,48},{48,32},{64,80},{80,64},{96,112},{112,96},{1... | collective-permute-start | bytes 2457608 | tf_op jit(solution)/shard_map/cond/branch_0_fun/ppermute | solution.py:19
  379.4 17.3 %collective-permute-start.1 = (bf16[1]{0:T(256)(128)(2,1)}, bf16[1]{0:T(256)(128)(2,1)}, u32[]{:S(2)}, u32[]{:S(2)}) collective-permute-start(bf16[1]{0:T(256)(128)(2,1)} %convert_element_type.72), channel_id=1, source_target_pairs={{0,16},{16,0},{32,48},{48,32},{64,80},{80,64},{96,112},{112,96},{1... | collective-permute-start | bytes 14 | tf_op jit(solution)/shard_map/cond/branch_0_fun/ppermute | solution.py:19
  398.7 3.4 copy-start.1
Sparse Core Ops, SparseCore 0:
  11.3 146.1 all-gather.1
  197.2 175.8 reduce-scatter.3
where the time goes:
time: 411 us; the launch traced here: 410 us
  waiting for transfers between devices  315 us (77%)
  local copies, waits for them, and re-layouts  25.7 us (6%)
  matrix products  21.2 us (5%)
  starting transfers between devices  17.8 us (4%)
  between operations  16.8 us (4%)
  other arithmetic  11.9 us (3%)
    reduce_scatter x1, waiting for transfers between devices, on_device(): lax.psum_scatter(lax.dot_general(columns, dpre, (((0,), (0,)), ((), ())),...  175 us
    all_gather x1, waiting for transfers between devices, on_device(): lax.all_gather(weight_rows, 'shard', axis=0, tiled=True)  139 us
    unnamed x13, local copies, waits for them, and re-layouts  25.7 us
    ppermute x2, starting transfers between devices, from_partner(): lax.ppermute(shard, axis, [(i, i ^ 1 << apart) for i in range(lax.axis_si...  17.8 us
    dot_general x1, matrix products, on_device(): jnp.dot(columns, lax.all_gather(weight_rows, 'shard', axis=0, tiled=True)...  10.8 us
    dot_general x1, matrix products, on_device(): lax.dot_general(columns, dpre, (((0,), (0,)), ((), ())), preferred_elemen...  10.4 us
  transfers between devices with their start and end apart: 4, of which 3 were waited for; matrix products, arithmetic and copies ran while one was open for 2% of the time, Pallas kernels for 0%

commit v1 on v0

--- a/solution.py
+++ b/solution.py
@@ -25,7 +25,9 @@
     columns = acts
     pre = resid[0].astype(jnp.float32) + jnp.dot(
         columns,
-        lax.all_gather(weight_rows, "shard", axis=0, tiled=True),
+        jnp.concatenate(
+            lax.all_to_all(jnp.stack([weight_rows] * lax.axis_size("shard")), "shard", 0, 0), axis=0
+        ),
         preferred_element_type=jnp.float32,
     )
     inv = lax.rsqrt(jnp.mean(pre * pre, axis=1, keepdims=True) + EPS)

time: 411 us -> 666 us (1.62)
  waiting for transfers between devices: 315 us -> 545 us
  local copies, waits for them, and re-layouts: 25.7 us -> 43.1 us
  starting transfers between devices: 17.8 us -> 28.2 us
    all_to_all x0 -> x1, waiting for transfers between devices: none -> 326 us  [on_device(): lax.all_to_all(jnp.stack([weight_rows] * lax.axis_size('shard')), 'shard'...]
    unnamed x2, waiting for transfers between devices: 0.03 us -> 218 us
    reduce_scatter x1 -> x0, waiting for transfers between devices: 175 us -> none  [on_device(): lax.psum_scatter(lax.dot_general(columns, dpre, (((0,), (0,)), ((), ())),...]
    all_gather x1 -> x0, waiting for transfers between devices: 139 us -> none  [on_device(): lax.all_gather(weight_rows, 'shard', axis=0, tiled=True)]
    all_to_all x0 -> x1, starting transfers between devices: none -> 10.3 us  [on_device(): lax.all_to_all(jnp.stack([weight_rows] * lax.axis_size('shard')), 'shard'...]
    unnamed x13 -> x17, local copies, waits for them, and re-layouts: 25.7 us -> 35.1 us
    another operation x0 -> x2, local copies, waits for them, and re-layouts: none -> 7.93 us  [the longest x1 6.01 us: on_device(): jnp.stack([weight_rows] * lax.axis_size('shard'))]
where the time goes in v1:
time: 666 us; the launch traced here: 665 us
  waiting for transfers between devices  545 us (82%)
  local copies, waits for them, and re-layouts  43.1 us (6%)
  starting transfers between devices  28.2 us (4%)
  matrix products  21.2 us (3%)
  between operations  16.7 us (3%)
  other arithmetic  9.3 us (1%)
    all_to_all x1, waiting for transfers between devices, on_device(): lax.all_to_all(jnp.stack([weight_rows] * lax.axis_size('shard')), 'shard'...  326 us
    unnamed x2, waiting for transfers between devices  218 us
    unnamed x17, local copies, waits for them, and re-layouts  35.1 us
    ppermute x2, starting transfers between devices, from_partner(): lax.ppermute(shard, axis, [(i, i ^ 1 << apart) for i in range(lax.axis_si...  17.8 us
  transfers between devices with their start and end apart: 4, of which 3 were waited for; matrix products, arithmetic and copies ran while one was open for 2% of the time, Pallas kernels for 0%

profile of v1, /device:TPU:32, one launch (start us, length us, event | category | flops | bytes accessed | tf_op | source)
XLA Modules:
  0.0 665.1 jit_solution(12232773841988195577)
XLA Ops:
  8.0 1.5 fusion.16
  9.5 6.0 stack.5
  15.5 10.3 %all-to-all-start = ((bf16[16,160,2560]{2,1,0:T(8,128)(2,1)}), bf16[16,160,2560]{2,1,0:T(8,128)(2,1)}, u32[]{:S(2)}, u32[]{:S(2)}) async-start(bf16[16,160,2560]{2,1,0:T(8,128)(2,1)} %stack.5), calls=%async_computation | async-start | bytes 26214400 | tf_op jit(solution)/shard_map/all_to_all | solution.py:29
  25.9 0.0 reduce-scatter.4.cloned.1.call-start
  25.9 4.0 copy.19
  29.9 4.1 copy.20
  34.0 325.6 %all-to-all-done = bf16[16,160,2560]{2,1,0:T(8,128)(2,1)} async-done(((bf16[16,160,2560]{2,1,0:T(8,128)(2,1)}), bf16[16,160,2560]{2,1,0:T(8,128)(2,1)}, u32[]{:S(2)}, u32[]{:S(2)}) %all-to-all-start) | async-done | bytes 13107232 | tf_op jit(solution)/shard_map/all_to_all | solution.py:29
  359.6 10.8 %multiply_reduce_fusion = (f32[384]{0:T(512)S(1)}, f32[384,2560]{0,1:T(8,128)S(1)}) fusion(bf16[2560,2560]{1,0:T(8,128)(2,1)} %bitcast.4, bf16[1,384,2560]{2,1,0:T(8,128)(2,1)S(1)} %copy-done, bf16[1,384,2560]{1,2,0:T(8,128)(2,1)} %copy.19), kind=kOutput, calls=%fused_computation.10 | convolution fusion | flops 5037096448 | bytes 20973056 | tf_op jit(solution)/shard_map/dot_general | solution.py:26
  370.4 0.7 fusion.4
  371.1 10.4 %fusion = bf16[2560,2560]{0,1:T(8,128)(2,1)} fusion(f32[384,2560]{0,1:T(8,128)S(1)} %get-tuple-element.68, bf16[1,384,2560]{1,2,0:T(8,128)(2,1)S(1)} %copy-done.2, bf16[1,384,2560]{2,1,0:T(8,128)(2,1)S(1)} %copy-done, f32[384]{0:T(512)S(1)} %broadcast_multiply_fusion, f32[2560]{0:T(1024)S(1)} %copy-done.4, f32[384]{0:T(512)S(1)} %add_rsqrt_fusion), kind=kOutput, calls=%fused_computation.1 | convolution fusion | flops 5046599680 | bytes 20984832 | tf_op jit(solution)/shard_map/dot_general | solution.py:41
  381.6 17.6 %copy.27 = bf16[2560,2560]{1,0:T(8,128)(2,1)} copy(bf16[2560,2560]{0,1:T(8,128)(2,1)} %fusion) | data formatting | bytes 26214400
  399.2 1.4 copy-done.3
  400.6 2.0 copy.18
  403.3 218.4 %reduce-scatter.4.cloned.1.call-done = bf16[160,2560]{1,0:T(8,128)(2,1)} async-done(((bf16[2560,2560]{1,0:T(8,128)(2,1)}), bf16[160,2560]{1,0:T(8,128)(2,1)}) %reduce-scatter.4.cloned.1.call-update) | async-done | bytes 819216
  621.7 1.5 copy.28
  623.2 3.5 bitcast_subtract_fusion
  626.7 22.4 %conditional.4 = (bf16[160,2560]{1,0:T(8,128)(2,1)}, f32[1]{0:T(128)}) conditional(s32[]{:T(128)} %bitcast.9, (f32[160,2560]{0,1:T(8,128)}, f32[1]{0:T(128)}) %tuple.50, (f32[160,2560]{0,1:T(8,128)}, f32[1]{0:T(128)}) %tuple.50, (f32[160,2560]{0,1:T(8,128)}, f32[1]{0:T(128)}) %tuple.50, (f32[160,2560]{0,1:T(8,128)}, ...), branch_computations={%region_3.0_spmd, %region_4.0_spmd, %region_5.0_spmd, %region_6.0_... | conditional | flops 2 | bytes 5734516
  626.7 1.9 copy.21
  628.6 1.6 collective-permute-start
  630.8 16.2 %collective-permute-start.1 = (bf16[1]{0:T(256)(128)(2,1)}, bf16[1]{0:T(256)(128)(2,1)}, u32[]{:S(2)}, u32[]{:S(2)}) collective-permute-start(bf16[1]{0:T(256)(128)(2,1)} %convert_element_type.73), channel_id=1, source_target_pairs={{0,16},{16,0},{32,48},{48,32},{64,80},{80,64},{96,112},{112,96},{1... | collective-permute-start | bytes 14 | tf_op jit(solution)/shard_map/cond/branch_0_fun/ppermute | solution.py:19
  647.1 1.0 collective-permute-done.1
  649.0 1.5 copy.25
  650.6 3.6 fusion.8
  654.2 3.0 copy.26
  (13 shorter events, 0.1 us)
Async XLA Ops:
  7.2 352.4 %copy-start = (bf16[1,384,2560]{2,1,0:T(8,128)(2,1)S(1)}, bf16[1,384,2560]{2,1,0:T(8,128)(2,1)}, u32[]{:S(2)}) copy-start(bf16[1,384,2560]{2,1,0:T(8,128)(2,1)} %param.11) | copy-start | bytes 5898244
  15.5 344.1 %all-to-all-start = ((bf16[16,160,2560]{2,1,0:T(8,128)(2,1)}), bf16[16,160,2560]{2,1,0:T(8,128)(2,1)}, u32[]{:S(2)}, u32[]{:S(2)}) async-start(bf16[16,160,2560]{2,1,0:T(8,128)(2,1)} %stack.5), calls=%async_computation | async-start | bytes 26214400 | tf_op jit(solution)/shard_map/all_to_all | solution.py:29
  25.9 595.8 %reduce-scatter.4.cloned.1.call-start = ((), (), s32[]{:S(2)}) async-start(), calls=%async_computation.2 | async-start | bytes 13926400
  359.6 10.8 %copy-start.2 = (bf16[1,384,2560]{1,2,0:T(8,128)(2,1)S(1)}, bf16[1,384,2560]{1,2,0:T(8,128)(2,1)}, u32[]{:S(2)}) copy-start(bf16[1,384,2560]{1,2,0:T(8,128)(2,1)} %copy.20) | copy-start | bytes 5898244
  359.6 10.8 %copy-start.4 = (f32[2560]{0:T(1024)S(1)}, f32[2560]{0:T(1024)}, u32[]{:S(2)}) copy-start(f32[2560]{0:T(1024)} %param.14) | copy-start | bytes 30724
  399.2 1.4 copy-start.3
  628.6 20.2 %collective-permute-start = (bf16[160,2560]{1,0:T(8,128)(2,1)S(1)}, bf16[160,2560]{1,0:T(8,128)(2,1)}, u32[]{:S(2)}, u32[]{:S(2)}) collective-permute-start(bf16[160,2560]{1,0:T(8,128)(2,1)S(1)} %copy.21), channel_id=1, source_target_pairs={{0,16},{16,0},{32,48},{48,32},{64,80},{80,64},{96,112},{112,96},{1... | collective-permute-start | bytes 2457608 | tf_op jit(solution)/shard_map/cond/branch_0_fun/ppermute | solution.py:19
  630.8 17.3 %collective-permute-start.1 = (bf16[1]{0:T(256)(128)(2,1)}, bf16[1]{0:T(256)(128)(2,1)}, u32[]{:S(2)}, u32[]{:S(2)}) collective-permute-start(bf16[1]{0:T(256)(128)(2,1)} %convert_element_type.73), channel_id=1, source_target_pairs={{0,16},{16,0},{32,48},{48,32},{64,80},{80,64},{96,112},{112,96},{1... | collective-permute-start | bytes 14 | tf_op jit(solution)/shard_map/cond/branch_0_fun/ppermute | solution.py:19
  650.6 6.6 copy-start.1
Sparse Core Ops, SparseCore 0:
  399.3 222.3 reduce-scatter.3
